TPU v7x, 32 devices: a whole 2x2x4 slice. The times are simulated.
32 devices in a mesh: shot: 4 (over y, core), mesh: 8 (over z, x).
Axes of the slice: x: 2, y: 2, z: 4, core: 2. Of those that a mesh axis runs over, the one named last changes fastest.
Arguments:
- adjoint_state: float32 [4, 13, 35, 1024], P('shot', None, None, 'mesh'), may hold values from -6 to 6
- forward_states: float32 [4, 2, 13, 35, 1024], P('shot', None, None, None, 'mesh'), may hold values from -6 to 6
- material: float32 [6, 35, 1024], P(None, None, 'mesh'), may hold values from 0.5 to 2
- coupling: float32 [3, 6, 13, 13], replicated, may hold values from -0.375 to 0.375
- metric: float32 [3, 3, 1024], P(None, None, 'mesh'), may hold values from -4 to 4
- face_normals: float32 [3, 4, 1024], P(None, None, 'mesh'), may hold values from -4 to 4
- face_scale: float32 [4, 1024], P(None, 'mesh'), may hold values from 1 to 3
- face_neighbours: int32 [4, 1024], P(None, 'mesh'), may hold values from 0 to 639, as said below
- face_orientation: int32 [4, 1024], P(None, 'mesh'), may hold values from 0 to 5
- send_faces: int32 [1024], P('mesh'), may hold values from 0 to 511, as said below
- history_steps: float32 [5, 6, 35, 1024], P(None, None, None, 'mesh')
- history_changes: float32 [5, 6, 35, 1024], P(None, None, None, 'mesh'), as said below
Outputs:
- adjoint_final: float32 [4, 13, 35, 1024], P('shot', None, None, 'mesh')
- direction: float32 [6, 35, 1024], P(None, None, ('mesh', 'shot'))
Inputs may be any that keep to these rules, and one draw needn't show every extreme that they name: `face_neighbours`: local faces of a partition are numbered x * 128 + e. Each face either forms a pair with another local face (each names the other) or reads exactly one of the 128 ghost slots, and every ghost slot is read by exactly one face; on every partition the face that reads slot 512 + j is send_faces[j] and the face that reads slot 576 + j is send_faces[64 + j]. `send_faces`: the 128 entries of one partition are distinct local face numbers. `history_changes`: for every stored pair, s_i . y_i is positive.
All inputs are finite; a program needn't handle non-finite values.
Results may differ from a plain program's by a relative error of at most 0.0003.
Values sent between devices are 32-bit elements; how exact they have to be, the bound alone decides.
No kernel may reach another device: no remote copies, remote signals or barrier semaphores. Data moves between devices by JAX's collectives and lax.ppermute only.
A program may use at most 64 MiB of HBM per device.

v0:
```python
import math
import jax
import jax.numpy as jnp
import numpy as np
from jax import lax
from jax.sharding import PartitionSpec as P

HIGH = lax.Precision.HIGHEST
STEP_SIZE = 0.02


def padded(x, sides, width):
    for axis, dim in sides:
        devices, length = (lax.axis_size(axis), x.shape[dim])
        up = [(i, (i + 1) % devices) for i in range(devices - 1)]
        down = [(j, i) for i, j in up]
        last = lax.slice_in_dim(x, length - width, length, axis=dim)
        first = lax.slice_in_dim(x, 0, width, axis=dim)
        before = lax.ppermute(last, axis, up)
        after = lax.ppermute(first, axis, down)
        x = jnp.concatenate([before, x, after], axis=dim)
    return x


def invert_matrix(matrix):
    order_count = matrix.shape[0]
    working = np.concatenate([matrix * 1.0, np.eye(order_count)], axis=1)
    for column in range(order_count):
        pivot_row = column + int(np.argmax(np.abs(working[column:, column])))
        working[[column, pivot_row]] = working[[pivot_row, column]]
        working[column] = working[column] / working[column, column]
        for target in range(order_count):
            if target != column:
                working[target] = working[target] - working[target, column] * working[column]
    return working[:, order_count:]


def basis_tables():
    points = [
        (across, along, upward)
        for upward in range(5)
        for along in range(5 - upward)
        for across in range(5 - upward - along)
    ]
    exponents = np.array(points) * 1.0
    coords = exponents / 4.0
    vander = np.prod(coords[:, None, :] ** exponents[None, :, :], axis=2)
    inverse = invert_matrix(vander)
    derivs = []
    for direction_axis in range(3):
        lowered = np.maximum(exponents - np.eye(3)[direction_axis], 0.0)
        slopes = exponents[None, :, direction_axis] * np.prod(
            coords[:, None, :] ** lowered[None, :, :], axis=2
        )
        derivs.append(slopes @ inverse)
    moments = np.array(
        [
            [
                math.factorial(first[0] + second[0])
                * math.factorial(first[1] + second[1])
                * math.factorial(first[2] + second[2])
                / math.factorial(sum(first) + sum(second) + 3)
                for second in points
            ]
            for first in points
        ]
    )
    mass_matrix = inverse.T @ moments @ inverse
    lattice = [(across, along) for along in range(5) for across in range(5 - along)]
    lattice_powers = np.array(lattice) * 1.0
    face_vander = np.prod((lattice_powers / 4.0)[:, None, :] ** lattice_powers[None, :, :], axis=2)
    face_inverse = invert_matrix(face_vander)
    face_moments = np.array(
        [
            [
                math.factorial(first[0] + second[0])
                * math.factorial(first[1] + second[1])
                / math.factorial(sum(first) + sum(second) + 2)
                for second in lattice
            ]
            for first in lattice
        ]
    )
    face_mass = face_inverse.T @ face_moments @ face_inverse
    numbers = {point: number for number, point in enumerate(points)}
    face_points = [
        [(across, along, 0) for across, along in lattice],
        [(across, 0, along) for across, along in lattice],
        [(0, across, along) for across, along in lattice],
        [(across, along, 4 - across - along) for across, along in lattice],
    ]
    face_nodes = np.array(
        [[numbers[point] for point in listing] for listing in face_points], np.int32
    )
    mass_inverse = invert_matrix(mass_matrix)
    lift_tables = []
    for face_number in range(4):
        selector = np.eye(35)[face_nodes[face_number]]
        lift_tables.append(mass_inverse @ selector.T @ face_mass)
    orderings = [(0, 1, 2), (1, 2, 0), (2, 0, 1), (1, 0, 2), (0, 2, 1), (2, 1, 0)]
    lattice_numbers = {point: number for number, point in enumerate(lattice)}
    triples = [(across, along, 4 - across - along) for across, along in lattice]
    turn_nodes = np.array(
        [
            [lattice_numbers[triple[ordering[0]], triple[ordering[1]]] for triple in triples]
            for ordering in orderings
        ],
        np.int32,
    )
    return (
        jnp.asarray(np.stack(derivs), jnp.float32),
        jnp.asarray(np.stack(lift_tables), jnp.float32),
        face_nodes,
        turn_nodes,
    )


def spatial_of(field, metric, derivs):
    reference_grads = jnp.einsum("rab,fbe->rfae", derivs, field, precision=HIGH)
    rows = []
    for direction_axis in range(3):
        total = metric[0, direction_axis] * reference_grads[0]
        total = total + metric[1, direction_axis] * reference_grads[1]
        total = total + metric[2, direction_axis] * reference_grads[2]
        rows.append(total)
    return jnp.stack(rows)


def volume_term(adjoint, material, coupling, metric, derivs):
    spatial = spatial_of(adjoint, metric, derivs)
    mixing = jnp.einsum("dpfg,dfae->pgae", coupling, spatial, precision=HIGH)
    return jnp.sum(material[:, None] * mixing, axis=0)


def kernel_term(adjoint, forward, coupling, metric, derivs):
    spatial = spatial_of(forward, metric, derivs)
    mixing = jnp.einsum("dpfg,dgae->pfae", coupling, spatial, precision=HIGH)
    return jnp.sum(mixing * adjoint[None], axis=1)


def surface_term(jump_trace, face_material, face_normals, face_scale, coupling, lift_tables):
    weighted = face_normals[:, None, None] * jump_trace[None]
    mixing = jnp.einsum("dpfg,dfnxe->pgnxe", coupling, weighted, precision=HIGH)
    face_flux = 0.5 * jnp.sum(face_material[:, None] * mixing, axis=0) + 0.5 * jump_trace
    return jnp.einsum(
        "xan,fnxe->fae", lift_tables, face_flux * face_scale[None, None], precision=HIGH
    )


def search_direction(total_grad, step_rows, change_rows, combine_sums):
    pairs = step_rows.shape[0]
    summed = combine_sums(
        jnp.concatenate(
            [
                jnp.sum(step_rows * change_rows, axis=(1, 2, 3)),
                jnp.sum(change_rows[pairs - 1] * change_rows[pairs - 1])[None],
            ]
        )
    )
    curvature = summed[:pairs]
    alphas = [None] * pairs
    work = total_grad
    for slot in reversed(range(pairs)):
        alphas[slot] = combine_sums(jnp.sum(step_rows[slot] * work)) / curvature[slot]
        work = work - alphas[slot] * change_rows[slot]
    work = curvature[pairs - 1] / summed[pairs] * work
    for slot in range(pairs):
        beta_now = combine_sums(jnp.sum(change_rows[slot] * work)) / curvature[slot]
        work = work + (alphas[slot] - beta_now) * step_rows[slot]
    return -work


def shards(
    adjoint_state,
    forward_states,
    material,
    coupling,
    metric,
    face_normals,
    face_scale,
    face_neighbours,
    face_orientation,
    send_faces,
    history_steps,
    history_changes,
):
    derivs, lift_tables, face_nodes, turn_nodes = basis_tables()
    fields = adjoint_state.shape[1]
    elements = adjoint_state.shape[3]
    node_count = material.shape[1]
    params = material.shape[0]
    face_width = face_nodes.shape[1]
    border = send_faces.shape[0] // 2
    slot_count = 4 * elements + 2 * border
    adjoint = adjoint_state[0]
    face_material = material[:, face_nodes.T, :]
    neighbours = face_neighbours.reshape(-1)
    orient = face_orientation.reshape(-1)
    node_pick = jnp.zeros((face_width, 4 * elements), jnp.int32)
    for option in range(turn_nodes.shape[0]):
        node_pick = (
            node_pick
            + (orient == option).astype(jnp.int32)[None, :]
            * jnp.asarray(turn_nodes[option], jnp.int32)[:, None]
        )
    flat_index = (node_pick * slot_count + neighbours[None, :]).reshape(-1)
    gradient = jnp.zeros((params, node_count, elements), jnp.float32)
    for step_index in range(forward_states.shape[1]):
        inner_trace = adjoint[:, face_nodes.T, :]
        flat_trace = inner_trace.reshape(fields, face_width, 4 * elements)
        sent_traces = flat_trace[:, :, send_faces]
        extended = padded(sent_traces, (("mesh", 2),), border)
        ghosts = jnp.concatenate(
            [flat_trace, extended[:, :, :border], extended[:, :, 3 * border :]], axis=2
        )
        turned = ghosts.reshape(fields, face_width * slot_count)[:, flat_index]
        jump_trace = turned.reshape(fields, face_width, 4, elements) - inner_trace
        change = volume_term(adjoint, material, coupling, metric, derivs) + surface_term(
            jump_trace, face_material, face_normals, face_scale, coupling, lift_tables
        )
        adjoint = adjoint + STEP_SIZE * change
        gradient = gradient + STEP_SIZE * kernel_term(
            adjoint, forward_states[0, step_index], coupling, metric, derivs
        )
    total_grad = lax.psum(gradient, "shot")

    def combine_sums(values):
        return lax.psum(values, "mesh")

    result = search_direction(total_grad, history_steps, history_changes, combine_sums)
    share_width = elements // lax.axis_size("shot")
    result = lax.dynamic_slice_in_dim(result, lax.axis_index("shot") * share_width, share_width, 2)
    return (adjoint[None], result)


def solution(mesh):
    placed = (
        P("shot", None, None, "mesh"),
        P("shot", None, None, None, "mesh"),
        P(None, None, "mesh"),
        P(),
        P(None, None, "mesh"),
        P(None, None, "mesh"),
        P(None, "mesh"),
        P(None, "mesh"),
        P(None, "mesh"),
        P("mesh"),
        P(None, None, None, "mesh"),
        P(None, None, None, "mesh"),
    )
    return jax.shard_map(
        shards,
        mesh=mesh,
        in_specs=placed,
        out_specs=(P("shot", None, None, "mesh"), P(None, None, ("mesh", "shot"))),
        check_vma=False,
    )
```

profile of v0, /device:TPU:0, one launch (start us, length us, event | category | flops | bytes accessed | tf_op | source)
XLA Modules:
  0.0 404.9 jit_solution(5043594300675908869)
XLA Ops:
  9.8 3.6 copy.157
  13.5 3.8 gather_fusion.2
  17.4 2.4 fusion.84
  21.2 6.3 %collective-permute-start = (f32[13,15,64]{1,0,2:T(8,128)}, f32[13,15,64]{1,0,2:T(8,128)}, u32[]{:S(2)}, u32[]{:S(2)}) collective-permute-start(f32[13,15,64]{1,0,2:T(8,128)} %get-tuple-element.22), channel_id=1, source_target_pairs={{0,1},{1,2},{2,3},{3,4},{4,5},{5,6},{6,7},{8,9},{9,10},{10,11},{11... | collective-permute-start | bytes 149768 | tf_op jit(solution)/shard_map/ppermute | solution.py:19
  33.5 2.3 fusion.5
  40.8 7.6 %collective-permute-done = f32[13,15,64]{1,0,2:T(8,128)} collective-permute-done((f32[13,15,64]{1,0,2:T(8,128)}, f32[13,15,64]{1,0,2:T(8,128)}, u32[]{:S(2)}, u32[]{:S(2)}) %collective-permute-start) | collective-permute-done | bytes 49952 | tf_op jit(solution)/shard_map/ppermute | solution.py:19
  49.8 3.2 copy.160
  53.0 17.3 %gather_fusion.3 = f32[7680,13]{1,0:T(8,128)} fusion(f32[13,9600]{0,1:T(8,128)} %bitcast.349, s32[8192]{0:T(1024)S(1)} %pad_clamp_fusion), kind=kCustom, calls=%fused_computation.3 | custom fusion | bytes 829440 | tf_op jit(solution)/shard_map/gather | solution.py:216
  70.3 2.7 copy.161
  73.1 3.6 fusion.1
  81.2 3.6 copy.170
  84.8 3.9 gather_fusion.5
  92.2 5.8 %collective-permute-start.2 = (f32[13,15,64]{1,0,2:T(8,128)}, f32[13,15,64]{1,0,2:T(8,128)}, u32[]{:S(2)}, u32[]{:S(2)}) collective-permute-start(f32[13,15,64]{1,0,2:T(8,128)} %get-tuple-element.20), channel_id=1, source_target_pairs={{0,1},{1,2},{2,3},{3,4},{4,5},{5,6},{6,7},{8,9},{9,10},{10,11},{11... | collective-permute-start | bytes 149768 | tf_op jit(solution)/shard_map/ppermute | solution.py:19
  98.2 2.4 fusion.3
  100.7 2.3 fusion.4
  103.0 4.5 %collective-permute-done.3 = f32[13,15,64]{1,0,2:T(8,128)} collective-permute-done((f32[13,15,64]{1,0,2:T(8,128)S(1)}, f32[13,15,64]{1,0,2:T(8,128)}, u32[]{:S(2)}, u32[]{:S(2)}) %collective-permute-start.3) | collective-permute-done | bytes 49952 | tf_op jit(solution)/shard_map/ppermute | solution.py:20
  108.7 10.1 %collective-permute-done.2 = f32[13,15,64]{1,0,2:T(8,128)} collective-permute-done((f32[13,15,64]{1,0,2:T(8,128)}, f32[13,15,64]{1,0,2:T(8,128)}, u32[]{:S(2)}, u32[]{:S(2)}) %collective-permute-start.2) | collective-permute-done | bytes 49952 | tf_op jit(solution)/shard_map/ppermute | solution.py:19
  120.2 3.2 copy.173
  123.5 17.3 %gather_fusion.6 = f32[7680,13]{1,0:T(8,128)} fusion(f32[13,9600]{0,1:T(8,128)} %bitcast.348, s32[8192]{0:T(1024)S(1)} %pad_clamp_fusion), kind=kCustom, calls=%fused_computation.6 | custom fusion | bytes 829440 | tf_op jit(solution)/shard_map/gather | solution.py:216
  140.8 2.8 copy.174
  143.7 2.7 fusion
  150.6 31.2 %all-reduce.3.cloned.1.call-done = f32[6,35,128]{2,0,1:T(8,128)} async-done(((f32[6,35,128]{2,0,1:T(8,128)}), f32[6,35,128]{2,0,1:T(8,128)}) %all-reduce.3.cloned.1.call-update) | async-done | bytes 107536 | tf_op jit(solution)/shard_map/psum | solution.py:225
  183.3 22.0 %all-reduce = (f32[]{:T(128)}, f32[6]{0:T(128)S(1)}) all-reduce(f32[]{:T(128)} %multiply_reduce_fusion.1, f32[6]{0:T(128)S(1)} %pad_maximum_fusion.2), channel_id=1, replica_groups=mesh['shot'=4,'mesh'=8] {'mesh'}, use_global_device_ids=true, to_apply=%region_11.0 | all-reduce | flops 7 | bytes 56 | tf_op jit(solution)/shard_map/psum | solution.py:228
  208.8 17.8 %psum.87 = f32[]{:T(128)} all-reduce(f32[]{:T(128)} %fusion.63), channel_id=1, replica_groups=mesh['shot'=4,'mesh'=8] {'mesh'}, use_global_device_ids=true, to_apply=%region_13.0 | all-reduce | flops 1 | bytes 8 | tf_op jit(solution)/shard_map/psum | solution.py:228
  229.5 19.7 %psum.88 = f32[]{:T(128)} all-reduce(f32[]{:T(128)} %get-tuple-element.18), channel_id=1, replica_groups=mesh['shot'=4,'mesh'=8] {'mesh'}, use_global_device_ids=true, to_apply=%region_15.0 | all-reduce | flops 1 | bytes 8 | tf_op jit(solution)/shard_map/psum | solution.py:228
  251.2 17.8 %psum.89 = f32[]{:T(128)} all-reduce(f32[]{:T(128)} %fusion.47), channel_id=1, replica_groups=mesh['shot'=4,'mesh'=8] {'mesh'}, use_global_device_ids=true, to_apply=%region_17.0 | all-reduce | flops 1 | bytes 8 | tf_op jit(solution)/shard_map/psum | solution.py:228
  271.0 19.7 %psum.90 = f32[]{:T(128)} all-reduce(f32[]{:T(128)} %get-tuple-element.16), channel_id=1, replica_groups=mesh['shot'=4,'mesh'=8] {'mesh'}, use_global_device_ids=true, to_apply=%region_19.0 | all-reduce | flops 1 | bytes 8 | tf_op jit(solution)/shard_map/psum | solution.py:228
  294.1 17.8 %psum.91 = f32[]{:T(128)} all-reduce(f32[]{:T(128)} %fusion.36), channel_id=1, replica_groups=mesh['shot'=4,'mesh'=8] {'mesh'}, use_global_device_ids=true, to_apply=%region_21.0 | all-reduce | flops 1 | bytes 8 | tf_op jit(solution)/shard_map/psum | solution.py:228
  313.9 19.8 %psum.92 = f32[]{:T(128)} all-reduce(f32[]{:T(128)} %fusion.44), channel_id=1, replica_groups=mesh['shot'=4,'mesh'=8] {'mesh'}, use_global_device_ids=true, to_apply=%region_23.0 | all-reduce | flops 1 | bytes 8 | tf_op jit(solution)/shard_map/psum | solution.py:228
  335.7 17.7 %psum.93 = f32[]{:T(128)} all-reduce(f32[]{:T(128)} %get-tuple-element.14), channel_id=1, replica_groups=mesh['shot'=4,'mesh'=8] {'mesh'}, use_global_device_ids=true, to_apply=%region_25.0 | all-reduce | flops 1 | bytes 8 | tf_op jit(solution)/shard_map/psum | solution.py:228
  356.3 19.7 %psum.94 = f32[]{:T(128)} all-reduce(f32[]{:T(128)} %fusion.60), channel_id=1, replica_groups=mesh['shot'=4,'mesh'=8] {'mesh'}, use_global_device_ids=true, to_apply=%region_27.0 | all-reduce | flops 1 | bytes 8 | tf_op jit(solution)/shard_map/psum | solution.py:228
  378.1 17.7 %psum.95 = f32[]{:T(128)} all-reduce(f32[]{:T(128)} %get-tuple-element.12), channel_id=1, replica_groups=mesh['shot'=4,'mesh'=8] {'mesh'}, use_global_device_ids=true, to_apply=%region_29.0 | all-reduce | flops 1 | bytes 8 | tf_op jit(solution)/shard_map/psum | solution.py:228
  (147 shorter events, 43.0 us)
Async XLA Ops:
  7.2 174.6 %all-reduce.3.cloned.1.call-start = ((), (), s32[]{:S(2)}) async-start(), calls=%async_computation | async-start | bytes 286720 | tf_op jit(solution)/shard_map/psum | solution.py:225
  9.5 4.0 copy-start.35
  9.8 17.7 %copy-start.2 = (f32[5,6,35,128]{3,2,1,0:T(8,128)S(1)}, f32[5,6,35,128]{3,2,1,0:T(8,128)}, u32[]{:S(2)}) copy-start(f32[5,6,35,128]{3,2,1,0:T(8,128)} %param.37) | copy-start | bytes 1612804
  9.8 17.7 %copy-start.3 = (f32[5,6,35,128]{3,2,1,0:T(8,128)S(1)}, f32[5,6,35,128]{3,2,1,0:T(8,128)}, u32[]{:S(2)}) copy-start(f32[5,6,35,128]{3,2,1,0:T(8,128)} %param.36) | copy-start | bytes 1612804
  13.5 3.9 copy-start.23
  13.5 15.6 %copy-start.26 = (s32[4,128]{1,0:T(4,128)S(1)}, s32[4,128]{1,0:T(4,128)}, u32[]{:S(2)}) copy-start(s32[4,128]{1,0:T(4,128)} %param.34) | copy-start | bytes 6148
  17.3 11.8 %copy-start.27 = (s32[4,128]{1,0:T(4,128)S(1)}, s32[4,128]{1,0:T(4,128)}, u32[]{:S(2)}) copy-start(s32[4,128]{1,0:T(4,128)} %param.33) | copy-start | bytes 6148
  17.3 11.8 %copy-start.30 = (s32[15]{0:T(128)S(1)}, s32[15]{0:T(128)}, u32[]{:S(2)}) copy-start(s32[15]{0:T(128)} %constant.67.clone) | copy-start | bytes 184
  17.3 11.8 %copy-start.31 = (s32[15]{0:T(128)S(1)}, s32[15]{0:T(128)}, u32[]{:S(2)}) copy-start(s32[15]{0:T(128)} %constant.66.clone) | copy-start | bytes 184
  17.3 11.8 %copy-start.32 = (s32[15]{0:T(128)S(1)}, s32[15]{0:T(128)}, u32[]{:S(2)}) copy-start(s32[15]{0:T(128)} %constant.65.clone) | copy-start | bytes 184
  17.3 11.8 %copy-start.33 = (s32[15]{0:T(128)S(1)}, s32[15]{0:T(128)}, u32[]{:S(2)}) copy-start(s32[15]{0:T(128)} %constant.64.clone) | copy-start | bytes 184
  17.3 11.8 %copy-start.34 = (s32[15]{0:T(128)S(1)}, s32[15]{0:T(128)}, u32[]{:S(2)}) copy-start(s32[15]{0:T(128)} %constant.63.clone) | copy-start | bytes 184
  17.4 12.0 %copy-start.28 = (f32[4,128]{1,0:T(4,128)S(1)}, f32[4,128]{1,0:T(4,128)}, u32[]{:S(2)}) copy-start(f32[4,128]{1,0:T(4,128)} %param.32) | copy-start | bytes 6148
  17.4 12.0 %copy-start.1 = (f32[1,13,35,128]{3,0,2,1:T(1,128)S(1)}, f32[1,13,35,128]{3,0,2,1:T(1,128)}, u32[]{:S(2)}) copy-start(f32[1,13,35,128]{3,0,2,1:T(1,128)} %param.26) | copy-start | bytes 698884
  17.4 12.0 %copy-start.10 = (f32[3,35,35,1]{2,1,3,0:T(8,128)S(1)}, f32[3,35,35,1]{2,1,3,0:T(8,128)}, u32[]{:S(2)}) copy-start(f32[3,35,35,1]{2,1,3,0:T(8,128)} %constant.74) | copy-start | bytes 44104
  19.8 10.5 %copy-start.25 = (f32[3,3,128]{2,1,0:T(4,128)S(1)}, f32[3,3,128]{2,1,0:T(4,128)}, u32[]{:S(2)}) copy-start(f32[3,3,128]{2,1,0:T(4,128)} %param.30) | copy-start | bytes 13828
  19.8 10.5 %copy-start = (f32[6,35,128]{2,1,0:T(8,128)S(1)}, f32[6,35,128]{2,1,0:T(8,128)}, u32[]{:S(2)}) copy-start(f32[6,35,128]{2,1,0:T(8,128)} %param.28) | copy-start | bytes 322564
  19.8 10.5 %copy-start.16 = (f32[1,2,13,35,128]{4,1,3,2,0:T(2,128)S(1)}, f32[1,2,13,35,128]{4,1,3,2,0:T(2,128)}, u32[]{:S(2)}) copy-start(f32[1,2,13,35,128]{4,1,3,2,0:T(2,128)} %param.27) | copy-start | bytes 1397764
  19.8 19.8 %collective-permute-start.1 = (f32[13,15,64]{1,0,2:T(8,128)}, f32[13,15,64]{1,0,2:T(8,128)}, u32[]{:S(2)}, u32[]{:S(2)}) collective-permute-start(f32[13,15,64]{1,0,2:T(8,128)} %get-tuple-element.23), channel_id=1, source_target_pairs={{1,0},{2,1},{3,2},{4,3},{5,4},{6,5},{7,6},{9,8},{10,9},{11,10},{12... | collective-permute-start | bytes 149768 | tf_op jit(solution)/shard_map/ppermute | solution.py:20
  21.2 27.2 %collective-permute-start = (f32[13,15,64]{1,0,2:T(8,128)}, f32[13,15,64]{1,0,2:T(8,128)}, u32[]{:S(2)}, u32[]{:S(2)}) collective-permute-start(f32[13,15,64]{1,0,2:T(8,128)} %get-tuple-element.22), channel_id=1, source_target_pairs={{0,1},{1,2},{2,3},{3,4},{4,5},{5,6},{6,7},{8,9},{9,10},{10,11},{11... | collective-permute-start | bytes 149768 | tf_op jit(solution)/shard_map/ppermute | solution.py:19
  35.8 3.7 copy-start.24
  39.6 33.6 %copy-start.21 = (f32[3,4,128]{2,0,1:T(4,128)}, f32[3,4,128]{2,0,1:T(4,128)S(1)}, u32[]{:S(2)}) copy-start(f32[3,4,128]{2,0,1:T(4,128)S(1)} %copy.154) | copy-start | bytes 18436
  73.0 3.8 copy-start.8
  73.0 3.8 copy-start.19
  88.7 9.4 %copy-start.12 = (f32[3,13,35,128,1]{3,2,1,0,4:T(8,128)S(1)}, f32[3,13,35,128,1]{3,2,1,0,4:T(8,128)}, u32[]{:S(2)}) copy-start(f32[3,13,35,128,1]{3,2,1,0,4:T(8,128)} %maximum_bitcast_fusion.2) | copy-start | bytes 2096644
  88.7 9.4 %copy-start.14 = (f32[3,6,13,13]{3,2,1,0:T(8,128)S(1)}, f32[3,6,13,13]{3,2,1,0:T(8,128)}, u32[]{:S(2)}) copy-start(f32[3,6,13,13]{3,2,1,0:T(8,128)} %param.29) | copy-start | bytes 36508
  90.9 16.6 %collective-permute-start.3 = (f32[13,15,64]{1,0,2:T(8,128)S(1)}, f32[13,15,64]{1,0,2:T(8,128)}, u32[]{:S(2)}, u32[]{:S(2)}) collective-permute-start(f32[13,15,64]{1,0,2:T(8,128)S(1)} %get-tuple-element.21), channel_id=1, source_target_pairs={{1,0},{2,1},{3,2},{4,3},{5,4},{6,5},{7,6},{9,8},{10,9},{11,10},{12... | collective-permute-start | bytes 149768 | tf_op jit(solution)/shard_map/ppermute | solution.py:20
  92.2 26.7 %collective-permute-start.2 = (f32[13,15,64]{1,0,2:T(8,128)}, f32[13,15,64]{1,0,2:T(8,128)}, u32[]{:S(2)}, u32[]{:S(2)}) collective-permute-start(f32[13,15,64]{1,0,2:T(8,128)} %get-tuple-element.20), channel_id=1, source_target_pairs={{0,1},{1,2},{2,3},{3,4},{4,5},{5,6},{6,7},{8,9},{9,10},{10,11},{11... | collective-permute-start | bytes 149768 | tf_op jit(solution)/shard_map/ppermute | solution.py:19
  146.4 4.1 %copy-start.6 = (f32[1,6,35,128]{3,2,1,0:T(8,128)S(1)}, f32[1,6,35,128]{3,2,1,0:T(8,128)}, u32[]{:S(2)}) copy-start(f32[1,6,35,128]{3,2,1,0:T(8,128)} %get-tuple-element.69) | copy-start | bytes 322564
  146.5 81.4 %copy-start.4 = (f32[1,6,35,128]{3,2,1,0:T(8,128)S(1)}, f32[1,6,35,128]{3,2,1,0:T(8,128)}, u32[]{:S(2)}) copy-start(f32[1,6,35,128]{3,2,1,0:T(8,128)} %get-tuple-element.39) | copy-start | bytes 322564
  146.6 104.0 %copy-start.5 = (f32[1,6,35,128]{3,2,1,0:T(8,128)S(1)}, f32[1,6,35,128]{3,2,1,0:T(8,128)}, u32[]{:S(2)}) copy-start(f32[1,6,35,128]{3,2,1,0:T(8,128)} %get-tuple-element.72) | copy-start | bytes 322564
  146.6 123.8 %copy-start.7 = (f32[1,6,35,128]{3,2,1,0:T(8,128)S(1)}, f32[1,6,35,128]{3,2,1,0:T(8,128)}, u32[]{:S(2)}) copy-start(f32[1,6,35,128]{3,2,1,0:T(8,128)} %get-tuple-element.37) | copy-start | bytes 322564
  (9 other events, 26.3 us)
Sparse Core Ops, SparseCore 0:
  150.0 31.6 all-reduce.2
where the time goes:
time: 406 us; the launch traced here: 405 us
  blocking collectives  190 us (47%)
  local copies, waits for them, and re-layouts  81.3 us (20%)
  waiting for transfers between devices  53.4 us (13%)
  between operations  29.4 us (7%)
  matrix products  19.9 us (5%)
  other arithmetic  16.3 us (4%)
  starting transfers between devices  14.9 us (4%)
    psum x10, blocking collectives, combine_sums(): return lax.psum(values, 'mesh')  190 us
    gather x2, local copies, waits for them, and re-layouts, shards(): turned = ghosts.reshape(fields, face_width * slot_count)[:, flat_index]  34.6 us
    psum x1, waiting for transfers between devices, shards(): total_grad = lax.psum(gradient, 'shot')  31.2 us
    ppermute x2, waiting for transfers between devices, padded(): before = lax.ppermute(last, axis, up)  17.7 us
    ppermute x2, starting transfers between devices, padded(): before = lax.ppermute(last, axis, up)  12.1 us
    reshape x4, local copies, waits for them, and re-layouts, shards(): flat_trace = inner_trace.reshape(fields, face_width, 4 * elements)  8.56 us
  transfers between devices with their start and end apart: 5, of which 4 were waited for; matrix products, arithmetic and copies ran while one was open for 5% of the time, Pallas kernels for 0%

commit v1 on v0

--- a/solution.py
+++ b/solution.py
@@ -222,7 +222,7 @@
         gradient = gradient + STEP_SIZE * kernel_term(
             adjoint, forward_states[0, step_index], coupling, metric, derivs
         )
-    total_grad = lax.psum(gradient, "shot")
+    total_grad = jnp.sum(lax.all_gather(gradient, "shot"), axis=0)
 
     def combine_sums(values):
         return lax.psum(values, "mesh")

time: 406 us -> 363 us (0.89)
  waiting for transfers between devices: 53.4 us -> 21.5 us
  between operations: 29.4 us -> 15.9 us
  blocking collectives: 190 us -> 196 us
    psum x1 -> x0, waiting for transfers between devices: 31.2 us -> none  [shards(): total_grad = lax.psum(gradient, 'shot')]
    all_gather x0 -> x1, blocking collectives: none -> 7.02 us  [shards(): total_grad = jnp.sum(lax.all_gather(gradient, 'shot'), axis=0)]
  transfers between devices with their start and end apart: 5 -> 4, of which waited for: 4 -> 3; matrix products, arithmetic and copies ran while one was open for 5% -> 5% of each run, Pallas kernels for 0% -> 0%
where the time goes in v1:
time: 363 us; the launch traced here: 362 us
  blocking collectives  196 us (54%)
  local copies, waits for them, and re-layouts  79.6 us (22%)
  waiting for transfers between devices  21.5 us (6%)
  matrix products  18.4 us (5%)
  between operations  15.9 us (4%)
  other arithmetic  15.7 us (4%)
  starting transfers between devices  14.8 us (4%)
    psum x10, blocking collectives, combine_sums(): return lax.psum(values, 'mesh')  189 us
    gather x2, local copies, waits for them, and re-layouts, shards(): turned = ghosts.reshape(fields, face_width * slot_count)[:, flat_index]  34.6 us
    ppermute x2, waiting for transfers between devices, padded(): before = lax.ppermute(last, axis, up)  17 us
    ppermute x2, starting transfers between devices, padded(): before = lax.ppermute(last, axis, up)  12.2 us
    reshape x4, local copies, waits for them, and re-layouts, shards(): flat_trace = inner_trace.reshape(fields, face_width, 4 * elements)  8.56 us
  transfers between devices with their start and end apart: 4, of which 3 were waited for; matrix products, arithmetic and copies ran while one was open for 5% of the time, Pallas kernels for 0%

profile of v1, /device:TPU:0, one launch (start us, length us, event | category | flops | bytes accessed | tf_op | source)
XLA Modules:
  0.0 361.6 jit_solution(3339148320260790142)
XLA Ops:
  3.3 3.6 %copy.157 = f32[13,15,512]{1,0,2:T(8,128)} copy(f32[13,15,512]{2,1,0:T(8,128)S(1)} %reshape.294) | data formatting | bytes 798720 | tf_op jit(solution)/shard_map/reshape | solution.py:210
  7.5 3.0 gather_fusion.2
  12.9 6.3 %collective-permute-start = (f32[13,15,64]{1,0,2:T(8,128)}, f32[13,15,64]{1,0,2:T(8,128)}, u32[]{:S(2)}, u32[]{:S(2)}) collective-permute-start(f32[13,15,64]{1,0,2:T(8,128)} %get-tuple-element.24), channel_id=1, source_target_pairs={{0,1},{1,2},{2,3},{3,4},{4,5},{5,6},{6,7},{8,9},{9,10},{10,11},{11... | collective-permute-start | bytes 149768 | tf_op jit(solution)/shard_map/ppermute | solution.py:19
  33.2 6.9 %collective-permute-done = f32[13,15,64]{1,0,2:T(8,128)} collective-permute-done((f32[13,15,64]{1,0,2:T(8,128)}, f32[13,15,64]{1,0,2:T(8,128)}, u32[]{:S(2)}, u32[]{:S(2)}) %collective-permute-start) | collective-permute-done | bytes 49952 | tf_op jit(solution)/shard_map/ppermute | solution.py:19
  40.0 1.9 copy.158
  42.9 3.2 copy.160
  46.1 17.3 %gather_fusion.3 = f32[7680,13]{1,0:T(8,128)} fusion(f32[13,9600]{0,1:T(8,128)} %bitcast.313, s32[8192]{0:T(1024)S(1)} %pad_clamp_fusion), kind=kCustom, calls=%fused_computation.3 | custom fusion | bytes 829440 | tf_op jit(solution)/shard_map/gather | solution.py:216
  63.4 2.7 copy.161
  66.3 3.6 %fusion.1 = f32[13,15,4,128]{3,0,2,1:T(8,128)S(1)} fusion(f32[6,15,4,128]{3,0,2,1:T(8,128)} %bitcast.325, f32[13,15,4,128]{3,0,2,1:T(8,128)S(1)} %sub.44, f32[3,4,128]{2,0,1:T(4,128)S(1)} %copy.154, f32[3,6,13,13]{3,2,1,0:T(8,128)S(1)} %copy-done.10), kind=kOutput, calls=%fused_computation.10 | convolution fusion | flops 281748480 | bytes 1001352 | tf_op jit(solution)/shard_map/dpfg,dfnxe->pgnxe/dot_general | solution.py:143
  74.4 3.6 %copy.170 = f32[13,15,512]{1,0,2:T(8,128)} copy(f32[13,15,512]{2,1,0:T(8,128)S(1)} %reshape.297) | data formatting | bytes 798720 | tf_op jit(solution)/shard_map/reshape | solution.py:210
  78.0 3.9 %gather_fusion.5 = f32[128,13,15]{2,1,0:T(8,128)} fusion(f32[13,15,512]{1,0,2:T(8,128)} %copy.170, s32[1024]{0:T(1024)} %pad_clamp_fusion.1), kind=kCustom, calls=%fused_computation.5 | custom fusion | bytes 200192 | tf_op jit(solution)/shard_map/gather | solution.py:211
  81.9 2.2 fusion.65
  85.5 5.8 %collective-permute-start.2 = (f32[13,15,64]{1,0,2:T(8,128)}, f32[13,15,64]{1,0,2:T(8,128)}, u32[]{:S(2)}, u32[]{:S(2)}) collective-permute-start(f32[13,15,64]{1,0,2:T(8,128)} %get-tuple-element.22), channel_id=1, source_target_pairs={{0,1},{1,2},{2,3},{3,4},{4,5},{5,6},{6,7},{8,9},{9,10},{10,11},{11... | collective-permute-start | bytes 149768 | tf_op jit(solution)/shard_map/ppermute | solution.py:19
  92.2 2.4 fusion.3
  96.3 4.5 %collective-permute-done.3 = f32[13,15,64]{1,0,2:T(8,128)} collective-permute-done((f32[13,15,64]{1,0,2:T(8,128)S(1)}, f32[13,15,64]{1,0,2:T(8,128)}, u32[]{:S(2)}, u32[]{:S(2)}) %collective-permute-start.3) | collective-permute-done | bytes 49952 | tf_op jit(solution)/shard_map/ppermute | solution.py:20
  102.1 10.1 %collective-permute-done.2 = f32[13,15,64]{1,0,2:T(8,128)} collective-permute-done((f32[13,15,64]{1,0,2:T(8,128)}, f32[13,15,64]{1,0,2:T(8,128)}, u32[]{:S(2)}, u32[]{:S(2)}) %collective-permute-start.2) | collective-permute-done | bytes 49952 | tf_op jit(solution)/shard_map/ppermute | solution.py:19
  113.5 3.2 copy.173
  116.8 17.3 %gather_fusion.6 = f32[7680,13]{1,0:T(8,128)} fusion(f32[13,9600]{0,1:T(8,128)} %bitcast.312, s32[8192]{0:T(1024)S(1)} %pad_clamp_fusion), kind=kCustom, calls=%fused_computation.6 | custom fusion | bytes 829440 | tf_op jit(solution)/shard_map/gather | solution.py:216
  134.1 2.8 copy.174
  137.0 2.7 fusion
  140.7 1.8 fusion.2
  142.5 7.0 %all-gather = f32[24,35,128]{2,1,0:T(8,128)S(1)} all-gather(f32[6,35,128]{2,1,0:T(8,128)S(1)} %copy.186), channel_id=2, replica_groups=mesh['shot'=4,'mesh'=8] {'shot'}, dimensions={0}, use_global_device_ids=true | all-gather | bytes 537600 | tf_op jit(solution)/shard_map/all_gather | solution.py:225
  150.2 20.9 %all-reduce = (f32[]{:T(128)}, f32[6]{0:T(128)S(1)}) all-reduce(f32[]{:T(128)} %multiply_reduce_fusion.1, f32[6]{0:T(128)S(1)} %copy-done.33), channel_id=1, replica_groups=mesh['shot'=4,'mesh'=8] {'mesh'}, use_global_device_ids=true, to_apply=%region_11.0 | all-reduce | flops 7 | bytes 56 | tf_op jit(solution)/shard_map/psum | solution.py:228
  173.7 17.7 %psum.79 = f32[]{:T(128)} all-reduce(f32[]{:T(128)} %fusion.51), channel_id=1, replica_groups=mesh['shot'=4,'mesh'=8] {'mesh'}, use_global_device_ids=true, to_apply=%region_13.0 | all-reduce | flops 1 | bytes 8 | tf_op jit(solution)/shard_map/psum | solution.py:228
  193.4 19.7 %psum.80 = f32[]{:T(128)} all-reduce(f32[]{:T(128)} %get-tuple-element.20), channel_id=1, replica_groups=mesh['shot'=4,'mesh'=8] {'mesh'}, use_global_device_ids=true, to_apply=%region_15.0 | all-reduce | flops 1 | bytes 8 | tf_op jit(solution)/shard_map/psum | solution.py:228
  215.1 17.7 %psum.81 = f32[]{:T(128)} all-reduce(f32[]{:T(128)} %fusion.43), channel_id=1, replica_groups=mesh['shot'=4,'mesh'=8] {'mesh'}, use_global_device_ids=true, to_apply=%region_17.0 | all-reduce | flops 1 | bytes 8 | tf_op jit(solution)/shard_map/psum | solution.py:228
  234.8 19.7 %psum.82 = f32[]{:T(128)} all-reduce(f32[]{:T(128)} %get-tuple-element.18), channel_id=1, replica_groups=mesh['shot'=4,'mesh'=8] {'mesh'}, use_global_device_ids=true, to_apply=%region_19.0 | all-reduce | flops 1 | bytes 8 | tf_op jit(solution)/shard_map/psum | solution.py:228
  257.8 17.7 %psum.83 = f32[]{:T(128)} all-reduce(f32[]{:T(128)} %get-tuple-element.16), channel_id=1, replica_groups=mesh['shot'=4,'mesh'=8] {'mesh'}, use_global_device_ids=true, to_apply=%region_21.0 | all-reduce | flops 1 | bytes 8 | tf_op jit(solution)/shard_map/psum | solution.py:228
  277.6 19.7 %psum.84 = f32[]{:T(128)} all-reduce(f32[]{:T(128)} %fusion.42), channel_id=1, replica_groups=mesh['shot'=4,'mesh'=8] {'mesh'}, use_global_device_ids=true, to_apply=%region_23.0 | all-reduce | flops 1 | bytes 8 | tf_op jit(solution)/shard_map/psum | solution.py:228
  299.3 17.7 %psum.85 = f32[]{:T(128)} all-reduce(f32[]{:T(128)} %get-tuple-element.14), channel_id=1, replica_groups=mesh['shot'=4,'mesh'=8] {'mesh'}, use_global_device_ids=true, to_apply=%region_25.0 | all-reduce | flops 1 | bytes 8 | tf_op jit(solution)/shard_map/psum | solution.py:228
  319.9 19.7 %psum.86 = f32[]{:T(128)} all-reduce(f32[]{:T(128)} %fusion.50), channel_id=1, replica_groups=mesh['shot'=4,'mesh'=8] {'mesh'}, use_global_device_ids=true, to_apply=%region_27.0 | all-reduce | flops 1 | bytes 8 | tf_op jit(solution)/shard_map/psum | solution.py:228
  341.6 17.7 %psum.87 = f32[]{:T(128)} all-reduce(f32[]{:T(128)} %get-tuple-element.12), channel_id=1, replica_groups=mesh['shot'=4,'mesh'=8] {'mesh'}, use_global_device_ids=true, to_apply=%region_29.0 | all-reduce | flops 1 | bytes 8 | tf_op jit(solution)/shard_map/psum | solution.py:228
  (142 shorter events, 41.2 us)
Async XLA Ops:
  2.9 4.0 %copy-start.32 = (s32[128]{0:T(128)S(1)}, s32[128]{0:T(128)}, u32[]{:S(2)}) copy-start(s32[128]{0:T(128)} %param.35) | copy-start | bytes 1540
  3.2 15.9 %copy-start.1 = (f32[5,6,35,128]{3,2,1,0:T(8,128)S(1)}, f32[5,6,35,128]{3,2,1,0:T(8,128)}, u32[]{:S(2)}) copy-start(f32[5,6,35,128]{3,2,1,0:T(8,128)} %param.37) | copy-start | bytes 1612804
  3.3 16.6 %copy-start.2 = (f32[5,6,35,128]{3,2,1,0:T(8,128)S(1)}, f32[5,6,35,128]{3,2,1,0:T(8,128)}, u32[]{:S(2)}) copy-start(f32[5,6,35,128]{3,2,1,0:T(8,128)} %param.36) | copy-start | bytes 1612804
  6.9 14.8 %copy-start.3 = (f32[1,13,35,128]{3,0,2,1:T(1,128)S(1)}, f32[1,13,35,128]{3,0,2,1:T(1,128)}, u32[]{:S(2)}) copy-start(f32[1,13,35,128]{3,0,2,1:T(1,128)} %param.26) | copy-start | bytes 698884
  6.9 15.6 %copy-start = (f32[6,35,128]{2,1,0:T(8,128)S(1)}, f32[6,35,128]{2,1,0:T(8,128)}, u32[]{:S(2)}) copy-start(f32[6,35,128]{2,1,0:T(8,128)} %param.28) | copy-start | bytes 322564
  10.4 10.2 %copy-start.29 = (s32[4,128]{1,0:T(4,128)S(1)}, s32[4,128]{1,0:T(4,128)}, u32[]{:S(2)}) copy-start(s32[4,128]{1,0:T(4,128)} %param.34) | copy-start | bytes 6148
  10.5 10.2 %copy-start.30 = (s32[4,128]{1,0:T(4,128)S(1)}, s32[4,128]{1,0:T(4,128)}, u32[]{:S(2)}) copy-start(s32[4,128]{1,0:T(4,128)} %param.33) | copy-start | bytes 6148
  10.5 11.2 %copy-start.31 = (f32[4,128]{1,0:T(4,128)S(1)}, f32[4,128]{1,0:T(4,128)}, u32[]{:S(2)}) copy-start(f32[4,128]{1,0:T(4,128)} %param.32) | copy-start | bytes 6148
  10.5 11.2 %copy-start.6 = (f32[3,35,35,1]{2,1,3,0:T(8,128)S(1)}, f32[3,35,35,1]{2,1,3,0:T(8,128)}, u32[]{:S(2)}) copy-start(f32[3,35,35,1]{2,1,3,0:T(8,128)} %constant.74) | copy-start | bytes 44104
  10.5 12.0 %copy-start.28 = (f32[3,3,128]{2,1,0:T(4,128)S(1)}, f32[3,3,128]{2,1,0:T(4,128)}, u32[]{:S(2)}) copy-start(f32[3,3,128]{2,1,0:T(4,128)} %param.30) | copy-start | bytes 13828
  10.5 12.1 %copy-start.14 = (f32[1,2,13,35,128]{4,1,3,2,0:T(2,128)S(1)}, f32[1,2,13,35,128]{4,1,3,2,0:T(2,128)}, u32[]{:S(2)}) copy-start(f32[1,2,13,35,128]{4,1,3,2,0:T(2,128)} %param.27) | copy-start | bytes 1397764
  11.6 20.3 %collective-permute-start.1 = (f32[13,15,64]{1,0,2:T(8,128)}, f32[13,15,64]{1,0,2:T(8,128)}, u32[]{:S(2)}, u32[]{:S(2)}) collective-permute-start(f32[13,15,64]{1,0,2:T(8,128)} %get-tuple-element.25), channel_id=1, source_target_pairs={{1,0},{2,1},{3,2},{4,3},{5,4},{6,5},{7,6},{9,8},{10,9},{11,10},{12... | collective-permute-start | bytes 149768 | tf_op jit(solution)/shard_map/ppermute | solution.py:20
  12.9 27.2 %collective-permute-start = (f32[13,15,64]{1,0,2:T(8,128)}, f32[13,15,64]{1,0,2:T(8,128)}, u32[]{:S(2)}, u32[]{:S(2)}) collective-permute-start(f32[13,15,64]{1,0,2:T(8,128)} %get-tuple-element.24), channel_id=1, source_target_pairs={{0,1},{1,2},{2,3},{3,4},{4,5},{5,6},{6,7},{8,9},{9,10},{10,11},{11... | collective-permute-start | bytes 149768 | tf_op jit(solution)/shard_map/ppermute | solution.py:19
  22.6 2.6 copy-start.4
  26.9 5.0 %copy-start.27 = (f32[3,4,128]{2,1,0:T(4,128)S(1)}, f32[3,4,128]{2,1,0:T(4,128)}, u32[]{:S(2)}) copy-start(f32[3,4,128]{2,1,0:T(4,128)} %param.31) | copy-start | bytes 18436
  31.9 34.4 %copy-start.25 = (f32[3,4,128]{2,0,1:T(4,128)}, f32[3,4,128]{2,0,1:T(4,128)S(1)}, u32[]{:S(2)}) copy-start(f32[3,4,128]{2,0,1:T(4,128)S(1)} %copy.154) | copy-start | bytes 18436
  66.2 3.8 %copy-start.17 = (f32[4,35,15,1]{1,2,0,3:T(8,128)S(1)}, f32[4,35,15,1]{1,2,0,3:T(8,128)}, u32[]{:S(2)}) copy-start(f32[4,35,15,1]{1,2,0,3:T(8,128)} %constant.75) | copy-start | bytes 25204
  66.3 4.6 %copy-start.7 = (f32[3,35,35,1]{2,1,3,0:T(8,128)S(1)}, f32[3,35,35,1]{2,1,3,0:T(8,128)}, u32[]{:S(2)}) copy-start(f32[3,35,35,1]{2,1,3,0:T(8,128)} %constant.74) | copy-start | bytes 44104
  74.4 17.0 %copy-start.20 = (f32[128]{0:T(128)S(1)}, f32[128]{0:T(128)}, u32[]{:S(2)}) copy-start(f32[128]{0:T(128)} %copy-done.19) | copy-start | bytes 1540
  81.9 10.2 %copy-start.9 = (f32[3,13,35,128,1]{3,2,1,0,4:T(8,128)S(1)}, f32[3,13,35,128,1]{3,2,1,0,4:T(8,128)}, u32[]{:S(2)}) copy-start(f32[3,13,35,128,1]{3,2,1,0,4:T(8,128)} %maximum_bitcast_fusion.2) | copy-start | bytes 2096644
  81.9 10.3 %copy-start.11 = (f32[3,6,13,13]{3,2,1,0:T(8,128)S(1)}, f32[3,6,13,13]{3,2,1,0:T(8,128)}, u32[]{:S(2)}) copy-start(f32[3,6,13,13]{3,2,1,0:T(8,128)} %param.29) | copy-start | bytes 36508
  84.1 10.6 %copy-start.5 = (f32[6,35,128]{2,0,1:T(8,128)S(1)}, f32[6,35,128]{2,0,1:T(8,128)}, u32[]{:S(2)}) copy-start(f32[6,35,128]{2,0,1:T(8,128)} %copy-done.4) | copy-start | bytes 322564
  84.1 16.7 %collective-permute-start.3 = (f32[13,15,64]{1,0,2:T(8,128)S(1)}, f32[13,15,64]{1,0,2:T(8,128)}, u32[]{:S(2)}, u32[]{:S(2)}) collective-permute-start(f32[13,15,64]{1,0,2:T(8,128)S(1)} %get-tuple-element.23), channel_id=1, source_target_pairs={{1,0},{2,1},{3,2},{4,3},{5,4},{6,5},{7,6},{9,8},{10,9},{11,10},{12... | collective-permute-start | bytes 149768 | tf_op jit(solution)/shard_map/ppermute | solution.py:20
  85.5 26.7 %collective-permute-start.2 = (f32[13,15,64]{1,0,2:T(8,128)}, f32[13,15,64]{1,0,2:T(8,128)}, u32[]{:S(2)}, u32[]{:S(2)}) collective-permute-start(f32[13,15,64]{1,0,2:T(8,128)} %get-tuple-element.22), channel_id=1, source_target_pairs={{0,1},{1,2},{2,3},{3,4},{4,5},{5,6},{6,7},{8,9},{9,10},{10,11},{11... | collective-permute-start | bytes 149768 | tf_op jit(solution)/shard_map/ppermute | solution.py:19
  134.1 2.9 copy-start.12
  134.1 2.9 copy-start.15
  134.1 2.9 copy-start.26
  136.9 2.9 copy-start.18
  137.0 3.6 %copy-start.8 = (f32[3,13,35,128,1]{3,2,1,0,4:T(8,128)S(1)}, f32[3,13,35,128,1]{3,2,1,0,4:T(8,128)}, u32[]{:S(2)}) copy-start(f32[3,13,35,128,1]{3,2,1,0,4:T(8,128)} %maximum_bitcast_fusion.3) | copy-start | bytes 2096644
  139.7 2.7 copy-start.16
  139.8 10.4 %copy-start.33 = (f32[6]{0:T(128)S(1)}, f32[6]{0:T(128)}, u32[]{:S(2)}) copy-start(f32[6]{0:T(128)} %pad_maximum_fusion.2) | copy-start | bytes 76
  149.5 211.2 %copy-start.13 = (f32[6,35,128]{2,1,0:T(8,128)S(1)}, f32[6,35,128]{2,1,0:T(8,128)}, u32[]{:S(2)}) copy-start(f32[6,35,128]{2,1,0:T(8,128)} %slice_bitcast_fusion) | copy-start | bytes 322564
  (6 other events, 13.4 us)
